TPU v7x, 512 devices: a whole 4x8x8 slice. The times are simulated.
512 devices in a mesh: member: 16 (over x_lo, y), dp: 32 (over z, x_hi, core).
Axes of the slice: x: 4 (x_hi: 2, x_lo: 2; x = x_hi * 2 + x_lo), y: 8, z: 8, core: 2. Of those that a mesh axis runs over, the one named last changes fastest.
Arguments:
- inputs: bfloat16 [8192, 64], P('dp'), may hold values from -6 to 6
- observed: float32 [64, 8192], P('member', 'dp'), may hold values from -6 to 6
- noise: bfloat16 [2, 32, 64, 8192], P(None, None, 'member', 'dp'), may hold values from -4 to 4
- w_in: float32 [32, 64, 4096], P('member', None, 'dp'), may hold values from -0.75 to 0.75
- b_in: float32 [32, 4096], P('member', 'dp'), may hold values from -3 to 3
- w_out: float32 [32, 64, 4096], P('member', None, 'dp'), may hold values from -0.09375 to 0.09375
- b_out: float32 [32, 64], P('member'), may hold values from -3 to 3
Outputs:
- new_w_in: float32 [32, 64, 4096], P('member', None, 'dp')
- new_b_in: float32 [32, 4096], P('member', 'dp')
- new_w_out: float32 [32, 64, 4096], P('member', None, 'dp')
- new_b_out: float32 [32, 64], P('member')
All inputs are finite; a program needn't handle non-finite values.
Results may differ from a plain program's by a relative error of at most 0.00056.
Values may be sent and summed in bfloat16 or wider, within the bound.
No kernel may reach another device: no remote copies, remote signals or barrier semaphores. Data moves between devices by JAX's collectives and lax.ppermute only.
A program may use at most 64 MiB of HBM per device.

v0:
```python
import jax
import jax.numpy as jnp
from jax import lax
from jax.sharding import PartitionSpec as P

UPDATES = 2
ridge_level = 0.5


def solve_gain(gram, cross):
    eye = jnp.eye(gram.shape[0], dtype=gram.dtype)
    factor = jnp.linalg.cholesky(gram + ridge_level * eye)
    middle = lax.linalg.triangular_solve(factor, cross, left_side=True, lower=True)
    return lax.linalg.triangular_solve(factor, middle, left_side=True, lower=True, transpose_a=True)


def pack(w_in, b_in, w_out, b_out):
    n = w_in.shape[0]
    return jnp.concatenate(
        [w_in.reshape(n, -1), w_out.reshape(n, -1), b_in.reshape(n, -1), b_out.reshape(n, -1)],
        axis=1,
    )


def unpack(flat, f_in, hid, outs):
    n = flat.shape[0]
    a = f_in * hid
    b = a + outs * hid
    c = b + hid
    return (
        flat[:, :a].reshape(n, f_in, hid),
        flat[:, b:c].reshape(n, hid),
        flat[:, a:b].reshape(n, outs, hid),
        flat[:, c:].reshape(n, outs),
    )


def predict(inputs, own_flat, b_out, f_in, hid, outs):
    n = own_flat.shape[0]
    a = f_in * hid
    b = a + outs * hid
    rounded = own_flat[:, : b + hid].astype(jnp.bfloat16)
    gathered = lax.all_gather(rounded, "dp", axis=0, tiled=False)
    d = gathered.shape[0]
    w_in = gathered[:, :, :a].reshape(d, n, f_in, hid)
    w_out = gathered[:, :, a:b].reshape(d, n, outs, hid)
    b_in = gathered[:, :, b : b + hid]
    pre = jnp.einsum("sf,dnfh->nsdh", inputs, w_in, preferred_element_type=jnp.float32)
    pre = pre + jnp.transpose(b_in, (1, 0, 2)).astype(jnp.float32)[:, None, :, :]
    hidden = jnp.tanh(pre).astype(jnp.bfloat16)
    pred = jnp.einsum("dnoh,nsdh->nos", w_out, hidden, preferred_element_type=jnp.float32)
    return pred + b_out[:, :, None]


def on_device(inputs, observed, noise, w_in, b_in, w_out, b_out):
    per_device = w_in.shape[0]
    f_in, hid = (w_in.shape[1], w_in.shape[2])
    outs = w_out.shape[1]
    count = observed.shape[0] * lax.axis_size("member") * observed.shape[1] * lax.axis_size("dp")
    first = lax.axis_index("member") * per_device
    own = pack(w_in, b_in, w_out, b_out)
    whole = lax.all_gather(own, "member", axis=0, tiled=True)
    for update in range(UPDATES):
        own_b_out = own[:, -outs:]
        predicted = predict(inputs, own, own_b_out, f_in, hid, outs)
        collected = lax.all_to_all(predicted, "member", split_axis=1, concat_axis=0, tiled=True)
        mean_pred = jnp.mean(collected, axis=0)
        anomaly = (collected - mean_pred[None]).reshape(collected.shape[0], -1)
        misfit = (observed[None] + noise[update].astype(jnp.float32) - collected).reshape(
            collected.shape[0], -1
        )
        gram_part = lax.dot_general(
            anomaly, anomaly, (((1,), (1,)), ((), ())), precision=lax.Precision.HIGHEST
        )
        cross_part = lax.dot_general(
            anomaly, misfit, (((1,), (1,)), ((), ())), precision=lax.Precision.HIGHEST
        )
        gram, cross = lax.psum((gram_part, cross_part), ("member", "dp"))
        gain = solve_gain(gram / count, cross / count)
        if update + 1 < UPDATES:
            moved = lax.dot_general(
                gain, whole, (((0,), (0,)), ((), ())), precision=lax.Precision.HIGHEST
            )
            whole = whole + moved
            own = lax.dynamic_slice_in_dim(whole, first, per_device, 0)
        else:
            columns = lax.dynamic_slice_in_dim(gain, first, per_device, 1)
            moved = lax.dot_general(
                columns, whole, (((0,), (0,)), ((), ())), precision=lax.Precision.HIGHEST
            )
            own = own + moved
    return unpack(own, f_in, hid, outs)


def solution(mesh):
    placed = (
        P("dp", None),
        P("member", "dp"),
        P(None, None, "member", "dp"),
        P("member", None, "dp"),
        P("member", "dp"),
        P("member", None, "dp"),
        P("member", None),
    )
    return jax.shard_map(
        on_device,
        mesh=mesh,
        in_specs=placed,
        out_specs=(
            P("member", None, "dp"),
            P("member", "dp"),
            P("member", None, "dp"),
            P("member", None),
        ),
        check_vma=False,
    )
```

profile of v0, /device:TPU:1, one launch (start us, length us, event | category | flops | bytes accessed | tf_op | source)
XLA Modules:
  0.0 511.3 jit_solution(14198276268625181387)
XLA Ops:
  7.2 0.7 convert_bitcast_fusion.2
  7.9 0.8 convert.20
  8.8 0.8 convert.19
  9.6 0.7 pad_maximum_fusion
  10.4 1.0 copy_bitcast_fusion.2
  11.4 1.4 maximum_bitcast_fusion
  12.8 90.6 %all-gather.7.cloned.1.call-done = bf16[32,2,16512]{2,1,0:T(2,128)(2,1)} async-done(((bf16[1,2,16512]{2,1,0:T(2,128)(2,1)}), bf16[32,2,16512]{2,1,0:T(2,128)(2,1)}) %all-gather.7.cloned.1.call-update) | async-done | bytes 2113552 | tf_op jit(solution)/shard_map/all_gather | solution.py:43
  103.4 0.7 convert_bitcast_fusion.1
  104.1 2.9 fusion.60
  107.1 0.8 reshape.148
  107.9 0.8 reshape.147
  108.8 2.5 fusion.20
  111.3 0.7 copy.43
  112.1 6.6 %all-to-all-start = ((f32[2,64,256]{2,0,1:T(2,128)}), f32[2,64,256]{2,0,1:T(2,128)S(1)}, u32[]{:S(2)}, u32[]{:S(2)}) async-start(f32[2,64,256]{2,0,1:T(2,128)} %copy.43), calls=%async_computation | async-start | bytes 262144 | tf_op jit(solution)/shard_map/all_to_all | solution.py:66
  118.8 47.6 %all-gather.9.cloned.1.call-done = f32[16,2,16576]{2,1,0:T(2,128)} async-done(((f32[1,2,16576]{2,1,0:T(2,128)}), f32[16,2,16576]{2,1,0:T(2,128)}) %all-gather.9.cloned.1.call-update) | async-done | bytes 2121744 | tf_op jit(solution)/shard_map/all_gather | solution.py:62
  166.4 3.7 reshape.128
  170.2 0.3 convolution_bitcast_fusion.3
  170.4 0.3 convolution_bitcast_fusion.2
  170.7 107.1 %all-reduce.1 = (f32[32,32]{0,1:T(8,128)S(1)}, f32[32,32]{0,1:T(8,128)S(1)}) all-reduce(f32[32,32]{0,1:T(8,128)S(1)} %convolution_bitcast_fusion.3, f32[32,32]{0,1:T(8,128)S(1)} %convolution_bitcast_fusion.2), channel_id=1, replica_groups=mesh['member'=16,'dp'=32] {'member','dp'}, use_global_device_ids=true, to_apply=%region_1.0 | all-reduce | flops 2048 | bytes 16384 | tf_op jit(solution)/shard_map/psum | solution.py:78
  277.9 2.9 cholesky.44
  280.8 0.6 compare_reduce_fusion.1
  281.5 0.7 fusion.39
  282.1 2.4 custom-call.11
  284.6 0.2 fusion.46
  285.0 4.2 convolution_add_fusion
  289.1 0.7 fusion.35
  289.9 80.4 %all-gather.11.cloned.1.call-done = bf16[32,2,16512]{2,1,0:T(2,128)(2,1)} async-done(((bf16[1,2,16512]{2,1,0:T(2,128)(2,1)}), bf16[32,2,16512]{2,1,0:T(2,128)(2,1)}) %all-gather.11.cloned.1.call-update) | async-done | bytes 2113552 | tf_op jit(solution)/shard_map/all_gather | solution.py:43
  370.3 4.0 fusion.59
  374.4 2.6 reshape.116
  377.0 0.7 convert_bitcast_fusion
  377.8 1.6 reshape.149
  379.4 3.2 fusion.1
  382.6 0.8 fusion.17
  383.6 13.8 %all_to_all.30 = f32[2,64,256]{2,0,1:T(2,128)S(1)} all-to-all(f32[2,64,256]{2,0,1:T(2,128)S(1)} %copy.55), channel_id=1, replica_groups=mesh['member'=16,'dp'=32] {'member'}, dimensions={1} | all-to-all | bytes 262144 | tf_op jit(solution)/shard_map/all_to_all | solution.py:66
  397.5 0.2 convolution_bitcast_fusion.1
  397.8 0.3 convolution_bitcast_fusion
  398.0 96.0 %all-reduce = (f32[32,32]{0,1:T(8,128)S(1)}, f32[32,32]{0,1:T(8,128)S(1)}) all-reduce(f32[32,32]{0,1:T(8,128)S(1)} %convolution_bitcast_fusion.1, f32[32,32]{0,1:T(8,128)S(1)} %convolution_bitcast_fusion), channel_id=1, replica_groups=mesh['member'=16,'dp'=32] {'member','dp'}, use_global_device_ids=true, to_apply=%region_6.10 | all-reduce | flops 2048 | bytes 16384 | tf_op jit(solution)/shard_map/psum | solution.py:78
  494.1 2.9 cholesky.55
  497.1 0.6 compare_reduce_fusion
  497.7 0.7 fusion.40
  498.4 2.4 custom-call.13
  500.8 0.2 fusion.41
  501.0 0.2 fusion.43
  501.3 1.1 convolution_add_fusion.1
  502.4 0.6 slice.74
  503.0 0.6 slice.76
  503.5 0.6 copy.119
  504.2 0.6 copy.118
  (40 shorter events, 1.1 us)
Async XLA Ops:
  7.2 101.6 %copy-start = (bf16[256,64]{0,1:T(8,128)(2,1)S(1)}, bf16[256,64]{0,1:T(8,128)(2,1)}, u32[]{:S(2)}) copy-start(bf16[256,64]{0,1:T(8,128)(2,1)} %param.12) | copy-start | bytes 98308
  7.2 96.2 %all-gather.7.cloned.1.call-start = ((), (), s32[]{:S(2)}) async-start(), calls=%async_computation.2 | async-start | bytes 2179584 | tf_op jit(solution)/shard_map/all_gather | solution.py:43
  10.3 156.0 %all-gather.9.cloned.1.call-start = ((), (), s32[]{:S(2)}) async-start(), calls=%async_computation.3 | async-start | bytes 2263040 | tf_op jit(solution)/shard_map/all_gather | solution.py:62
  107.1 1.7 copy-start.4
  108.8 9.9 %copy-start.2 = (bf16[2,32,4,256]{3,2,1,0:T(4,128)(2,1)S(1)}, bf16[2,32,4,256]{3,2,1,0:T(4,128)(2,1)}, u32[]{:S(2)}) copy-start(bf16[2,32,4,256]{3,2,1,0:T(4,128)(2,1)} %param.14) | copy-start | bytes 393220
  112.1 58.0 %all-to-all-start = ((f32[2,64,256]{2,0,1:T(2,128)}), f32[2,64,256]{2,0,1:T(2,128)S(1)}, u32[]{:S(2)}, u32[]{:S(2)}) async-start(f32[2,64,256]{2,0,1:T(2,128)} %copy.43), calls=%async_computation | async-start | bytes 262144 | tf_op jit(solution)/shard_map/all_to_all | solution.py:66
  118.6 251.7 %all-gather.11.cloned.1.call-start = ((), (), s32[]{:S(2)}) async-start(), calls=%async_computation.4 | async-start | bytes 2179584 | tf_op jit(solution)/shard_map/all_gather | solution.py:43
  118.7 51.4 %copy-start.3 = (f32[4,256]{1,0:T(4,128)S(1)}, f32[4,256]{1,0:T(4,128)}, u32[]{:S(2)}) copy-start(f32[4,256]{1,0:T(4,128)} %param.13) | copy-start | bytes 12292
  379.4 3.2 copy-start.1
Sparse Core Ops, SparseCore 0:
  11.4 91.9 all-gather.6
  105.5 60.8 all-gather.8
  290.0 80.3 all-gather.10
where the time goes:
time: 512 us; the launch traced here: 511 us
  waiting for transfers between devices  219 us (43%)
  blocking collectives  217 us (42%)
  local copies, waits for them, and re-layouts  21.8 us (4%)
  other arithmetic  19.5 us (4%)
  between operations  14 us (3%)
  matrix products  13.7 us (3%)
  starting transfers between devices  6.69 us (1%)
    psum x2, blocking collectives, on_device(): gram, cross = lax.psum((gram_part, cross_part), ('member', 'dp'))  203 us
    all_gather x2, waiting for transfers between devices, predict(): gathered = lax.all_gather(rounded, 'dp', axis=0, tiled=False)  171 us
    all_gather x1, waiting for transfers between devices, on_device(): whole = lax.all_gather(own, 'member', axis=0, tiled=True)  47.6 us
    all_to_all x1, blocking collectives, on_device(): lax.all_to_all(predicted, 'member', split_axis=1, concat_axis=0, tiled=True)  13.8 us
  transfers between devices with their start and end apart: 4, of which 3 were waited for; matrix products, arithmetic and copies ran while one was open for 3% of the time, Pallas kernels for 0%

commit v1 on v0

--- a/solution.py
+++ b/solution.py
@@ -5,6 +5,11 @@
 
 UPDATES = 2
 ridge_level = 0.5
+
+
+def one_after_other(value, leading, second):
+    partial = lax.psum(value, leading)
+    return lax.psum(partial, second)
 
 
 def solve_gain(gram, cross):
@@ -75,7 +80,7 @@
         cross_part = lax.dot_general(
             anomaly, misfit, (((1,), (1,)), ((), ())), precision=lax.Precision.HIGHEST
         )
-        gram, cross = lax.psum((gram_part, cross_part), ("member", "dp"))
+        gram, cross = one_after_other((gram_part, cross_part), "member", "dp")
         gain = solve_gain(gram / count, cross / count)
         if update + 1 < UPDATES:
             moved = lax.dot_general(

time: 512 us -> 700 us (1.37)
  blocking collectives: 217 us -> 396 us
    psum x2 -> x4, blocking collectives: 203 us -> 382 us  [the longest x2 286 us: one_after_other(): return lax.psum(partial, second)]
  transfers between devices with their start and end apart: 4 -> 4, of which waited for: 3 -> 3; matrix products, arithmetic and copies ran while one was open for 3% -> 2% of each run, Pallas kernels for 0% -> 0%
where the time goes in v1:
time: 700 us; the launch traced here: 695 us
  blocking collectives  396 us (57%)
  waiting for transfers between devices  223 us (32%)
  local copies, waits for them, and re-layouts  21.9 us (3%)
  other arithmetic  19.5 us (3%)
  between operations  14 us (2%)
  matrix products  13.7 us (2%)
    psum x2, blocking collectives, one_after_other(): return lax.psum(partial, second)  286 us
    all_gather x2, waiting for transfers between devices, predict(): gathered = lax.all_gather(rounded, 'dp', axis=0, tiled=False)  176 us
    psum x2, blocking collectives, one_after_other(): partial = lax.psum(value, leading)  95.8 us
    all_gather x1, waiting for transfers between devices, on_device(): whole = lax.all_gather(own, 'member', axis=0, tiled=True)  47.7 us
  transfers between devices with their start and end apart: 4, of which 3 were waited for; matrix products, arithmetic and copies ran while one was open for 2% of the time, Pallas kernels for 0%

profile of v1, /device:TPU:1, one launch (start us, length us, event | category | flops | bytes accessed | tf_op | source)
XLA Modules:
  0.0 695.3 jit_solution(3234000855787882192)
XLA Ops:
  7.2 0.7 convert_bitcast_fusion.2
  7.9 0.8 convert.20
  8.8 0.8 convert.19
  9.6 0.7 pad_maximum_fusion
  10.4 1.0 copy_bitcast_fusion.2
  11.4 1.4 maximum_bitcast_fusion
  12.8 90.6 %all-gather.7.cloned.1.call-done = bf16[32,2,16512]{2,1,0:T(2,128)(2,1)} async-done(((bf16[1,2,16512]{2,1,0:T(2,128)(2,1)}), bf16[32,2,16512]{2,1,0:T(2,128)(2,1)}) %all-gather.7.cloned.1.call-update) | async-done | bytes 2113552 | tf_op jit(solution)/shard_map/all_gather | solution.py:48
  103.4 0.7 convert_bitcast_fusion.1
  104.1 2.9 fusion.60
  107.1 0.8 reshape.148
  107.9 0.8 reshape.147
  108.8 2.5 fusion.20
  111.3 0.8 copy.43
  112.1 6.6 all-to-all-start
  118.8 47.7 %all-gather.9.cloned.1.call-done = f32[16,2,16576]{2,1,0:T(2,128)} async-done(((f32[1,2,16576]{2,1,0:T(2,128)}), f32[16,2,16576]{2,1,0:T(2,128)}) %all-gather.9.cloned.1.call-update) | async-done | bytes 2121744 | tf_op jit(solution)/shard_map/all_gather | solution.py:67
  166.5 3.7 reshape.128
  170.3 0.2 convolution_bitcast_fusion.3
  170.6 0.3 convolution_bitcast_fusion.2
  170.8 48.1 %all-reduce.3 = (f32[32,32]{0,1:T(8,128)S(1)}, f32[32,32]{0,1:T(8,128)S(1)}) all-reduce(f32[32,32]{0,1:T(8,128)S(1)} %convolution_bitcast_fusion.3, f32[32,32]{0,1:T(8,128)S(1)} %convolution_bitcast_fusion.2), channel_id=1, replica_groups=mesh['member'=16,'dp'=32] {'member'}, use_global_device_ids=true, to_apply=%region_1.0 | all-reduce | flops 2048 | bytes 16384 | tf_op jit(solution)/shard_map/psum | solution.py:11
  218.9 148.0 %all-reduce.1 = (f32[32,32]{0,1:T(8,128)S(1)}, f32[32,32]{0,1:T(8,128)S(1)}) all-reduce(f32[32,32]{0,1:T(8,128)S(1)} %get-tuple-element.13, f32[32,32]{0,1:T(8,128)S(1)} %get-tuple-element.14), channel_id=1, replica_groups=mesh['member'=16,'dp'=32] {'dp'}, use_global_device_ids=true, to_apply=%region_2.0 | all-reduce | flops 2048 | bytes 16384 | tf_op jit(solution)/shard_map/psum | solution.py:12
  367.0 2.9 cholesky.44
  369.9 0.6 compare_reduce_fusion.1
  370.6 0.7 fusion.39
  371.2 2.4 custom-call.11
  374.1 4.2 convolution_add_fusion
  378.2 0.7 fusion.35
  379.0 85.1 %all-gather.11.cloned.1.call-done = bf16[32,2,16512]{2,1,0:T(2,128)(2,1)} async-done(((bf16[1,2,16512]{2,1,0:T(2,128)(2,1)}), bf16[32,2,16512]{2,1,0:T(2,128)(2,1)}) %all-gather.11.cloned.1.call-update) | async-done | bytes 2113552 | tf_op jit(solution)/shard_map/all_gather | solution.py:48
  464.2 4.1 fusion.59
  468.2 2.6 reshape.116
  470.9 0.7 convert_bitcast_fusion
  471.6 1.6 reshape.149
  473.2 3.2 fusion.1
  476.5 0.8 fusion.17
  477.4 13.8 %all_to_all.30 = f32[2,64,256]{2,0,1:T(2,128)S(1)} all-to-all(f32[2,64,256]{2,0,1:T(2,128)S(1)} %copy.55), channel_id=1, replica_groups=mesh['member'=16,'dp'=32] {'member'}, dimensions={1} | all-to-all | bytes 262144 | tf_op jit(solution)/shard_map/all_to_all | solution.py:71
  491.4 0.3 convolution_bitcast_fusion.1
  491.6 0.3 convolution_bitcast_fusion
  491.9 47.7 %all-reduce.2 = (f32[32,32]{0,1:T(8,128)S(1)}, f32[32,32]{0,1:T(8,128)S(1)}) all-reduce(f32[32,32]{0,1:T(8,128)S(1)} %convolution_bitcast_fusion.1, f32[32,32]{0,1:T(8,128)S(1)} %convolution_bitcast_fusion), channel_id=1, replica_groups=mesh['member'=16,'dp'=32] {'member'}, use_global_device_ids=true, to_apply=%region_8.12 | all-reduce | flops 2048 | bytes 16384 | tf_op jit(solution)/shard_map/psum | solution.py:11
  539.6 138.4 %all-reduce = (f32[32,32]{0,1:T(8,128)S(1)}, f32[32,32]{0,1:T(8,128)S(1)}) all-reduce(f32[32,32]{0,1:T(8,128)S(1)} %get-tuple-element.11, f32[32,32]{0,1:T(8,128)S(1)} %get-tuple-element.12), channel_id=1, replica_groups=mesh['member'=16,'dp'=32] {'dp'}, use_global_device_ids=true, to_apply=%region_9.13 | all-reduce | flops 2048 | bytes 16384 | tf_op jit(solution)/shard_map/psum | solution.py:12
  678.1 2.9 cholesky.55
  681.0 0.6 compare_reduce_fusion
  681.7 0.7 fusion.40
  682.3 2.4 custom-call.13
  685.0 0.2 fusion.43
  685.2 1.1 convolution_add_fusion.1
  686.4 0.6 slice.74
  686.9 0.6 slice.76
  687.5 0.6 copy.119
  688.1 0.6 copy.118
  (42 shorter events, 1.6 us)
Async XLA Ops:
  7.2 101.6 %copy-start = (bf16[256,64]{0,1:T(8,128)(2,1)S(1)}, bf16[256,64]{0,1:T(8,128)(2,1)}, u32[]{:S(2)}) copy-start(bf16[256,64]{0,1:T(8,128)(2,1)} %param.12) | copy-start | bytes 98308
  7.2 96.2 %all-gather.7.cloned.1.call-start = ((), (), s32[]{:S(2)}) async-start(), calls=%async_computation.2 | async-start | bytes 2179584 | tf_op jit(solution)/shard_map/all_gather | solution.py:48
  10.3 156.1 %all-gather.9.cloned.1.call-start = ((), (), s32[]{:S(2)}) async-start(), calls=%async_computation.3 | async-start | bytes 2263040 | tf_op jit(solution)/shard_map/all_gather | solution.py:67
  107.1 1.7 copy-start.4
  108.8 9.9 %copy-start.2 = (bf16[2,32,4,256]{3,2,1,0:T(4,128)(2,1)S(1)}, bf16[2,32,4,256]{3,2,1,0:T(4,128)(2,1)}, u32[]{:S(2)}) copy-start(bf16[2,32,4,256]{3,2,1,0:T(4,128)(2,1)} %param.14) | copy-start | bytes 393220
  112.1 58.1 %all-to-all-start = ((f32[2,64,256]{2,0,1:T(2,128)}), f32[2,64,256]{2,0,1:T(2,128)S(1)}, u32[]{:S(2)}, u32[]{:S(2)}) async-start(f32[2,64,256]{2,0,1:T(2,128)} %copy.43), calls=%async_computation | async-start | bytes 262144 | tf_op jit(solution)/shard_map/all_to_all | solution.py:71
  118.6 345.5 %all-gather.11.cloned.1.call-start = ((), (), s32[]{:S(2)}) async-start(), calls=%async_computation.4 | async-start | bytes 2179584 | tf_op jit(solution)/shard_map/all_gather | solution.py:48
  118.8 51.5 %copy-start.3 = (f32[4,256]{1,0:T(4,128)S(1)}, f32[4,256]{1,0:T(4,128)}, u32[]{:S(2)}) copy-start(f32[4,256]{1,0:T(4,128)} %param.13) | copy-start | bytes 12292
  473.2 3.2 copy-start.1
Sparse Core Ops, SparseCore 0:
  11.4 91.9 all-gather.6
  105.5 60.9 all-gather.8
  379.1 85.0 all-gather.10
